TPU v7x, 128 devices: a whole 4x4x4 slice. The times are simulated.
128 devices in a mesh: req: 8 (over z, core), mp: 16 (over x, y).
Axes of the slice: x: 4, y: 4, z: 4, core: 2. Of those that a mesh axis runs over, the one named last changes fastest.
Arguments:
- states: bfloat16 [8, 32, 16, 5120], P('req', None, 'mp'), may hold values from -6 to 6
- lengths: int32 [8, 4], replicated, may hold values from 1 to 509, as said below
- request_adapters: int32 [8, 4], replicated, may hold values from 0 to 7
- attention_norm_gain: float32 [5120], replicated, may hold values from 0.1 to 1.9
- query_weight: bfloat16 [5120, 4096], P(None, 'mp')
- key_weight: bfloat16 [5120, 1024], P(None, 'mp')
- value_weight: bfloat16 [5120, 1024], P(None, 'mp'), may hold values from -0.078125 to 0.078125
- output_weight: bfloat16 [4096, 5120], P('mp'), may hold values from -0.09375 to 0.09375
- adapter_down_attention: bfloat16 [5120, 384], replicated, may hold values from -0.078125 to 0.078125
- adapter_up_query: bfloat16 [128, 4096], P(None, 'mp'), may hold values from -0.5 to 0.5
- adapter_up_key_value: bfloat16 [2, 128, 1024], P(None, None, 'mp'), may hold values from -0.5 to 0.5
- adapter_down_output: bfloat16 [4096, 128], P('mp'), may hold values from -0.09375 to 0.09375
- adapter_up_output: bfloat16 [128, 5120], replicated, may hold values from -0.875 to 0.875
- feed_norm_gain: float32 [5120], replicated, may hold values from 0.1 to 1.9
- gate_up_weight: bfloat16 [2, 5120, 10240], P(None, 'req', 'mp'), may hold values from -0.078125 to 0.078125
- down_weight: bfloat16 [5120, 10240], P('req', 'mp'), may hold values from -0.0625 to 0.0625
- adapter_down_gate_up: bfloat16 [5120, 256], replicated, may hold values from -0.078125 to 0.078125
- adapter_up_gate_up: bfloat16 [2, 128, 10240], P(None, None, 'mp'), may hold values from -0.5 to 0.5
- adapter_down_feed: bfloat16 [10240, 128], P('mp'), may hold values from -0.0625 to 0.0625
- adapter_up_feed: bfloat16 [128, 5120], replicated, may hold values from -0.875 to 0.875
Outputs:
- layer_out: bfloat16 [8, 32, 16, 5120], P('req', None, 'mp')
Inputs may be any that keep to these rules, and one draw needn't show every extreme that they name: `lengths`: each request has at least one token; each row sums to at most 512, some row to exactly 512, and all rows together to exactly 2048; some request is 509 tokens long.
All inputs are finite; a program needn't handle non-finite values.
Results may differ from a plain program's by a relative error of at most 0.03.
Values may be sent and summed in bfloat16 or wider, within the bound.
No kernel may reach another device: no remote copies, remote signals or barrier semaphores. Data moves between devices by JAX's collectives and lax.ppermute only.
A program may use at most 128 MiB of HBM per device.

v0:
```python
import jax
import jax.numpy as jnp
from jax import lax
from jax.sharding import PartitionSpec as P

HEAD_SIZE = 128
ADAPTER_RANK = 16
WINDOW = 128
SINK = 4
EPSILON = 1e-05
ROPE_THETA = 1000000.0


def from_partner(shard, axis, stride):
    return lax.ppermute(shard, axis, [(i, i ^ 1 << stride) for i in range(lax.axis_size(axis))])


def slot_info(length_rows, adapter_rows, slot_ids):
    request_ends = jnp.cumsum(length_rows, axis=1, dtype=jnp.int32)
    starts = request_ends - length_rows
    count_req = length_rows.shape[1]
    request = jnp.sum(
        (slot_ids[:, None] >= request_ends).astype(jnp.int32), axis=1, dtype=jnp.int32
    )
    living = request < count_req
    matches = request[:, None] == jnp.arange(count_req, dtype=jnp.int32)[None, :]
    opening = jnp.sum(jnp.where(matches, starts, 0), axis=1, dtype=jnp.int32)
    position = jnp.where(living, slot_ids - opening, 0)
    segment = jnp.where(living, request, count_req + slot_ids)
    chosen = jnp.sum(jnp.where(matches, adapter_rows, 0), axis=1, dtype=jnp.int32)
    adapter_slot = jnp.where(living, chosen, -1)
    return (living, position, segment, adapter_slot)


def normalize(input_tokens, gain_vec):
    values = input_tokens.astype(jnp.float32)
    factor = lax.rsqrt(jnp.mean(values * values, axis=-1, keepdims=True) + EPSILON)
    return (values * factor * gain_vec).astype(jnp.bfloat16)


def adapter_select_mask(adapter_slot, adapter_column_count, adapter_rank_size):
    token_owner_request = jnp.arange(adapter_column_count, dtype=jnp.int32) // adapter_rank_size
    return (adapter_slot[:, None] == token_owner_request[None, :]).astype(jnp.float32)


def rotate(vectors, position):
    half_dim = vectors.shape[-1] // 2
    inverse = ROPE_THETA ** (-(jnp.arange(half_dim, dtype=jnp.float32) * (2.0 / vectors.shape[-1])))
    angles = position.astype(jnp.float32)[:, None] * inverse[None, :]
    cosine = jnp.cos(angles)[:, None, :]
    sine_part = jnp.sin(angles)[:, None, :]
    lower_half = vectors[..., :half_dim]
    upper_half = vectors[..., half_dim:]
    return jnp.concatenate(
        [
            lower_half * cosine - upper_half * sine_part,
            upper_half * cosine + lower_half * sine_part,
        ],
        axis=-1,
    )


def attend(queries, key_rows, value_rows, position, segment):
    key_heads = key_rows.shape[1]
    group_size = queries.shape[1] // key_heads
    token_count = queries.shape[0]
    grouped_queries = queries.reshape(token_count, key_heads, group_size, queries.shape[2])
    scores = jnp.einsum(
        "qkgd,skd->kgqs", grouped_queries, key_rows, preferred_element_type=jnp.float32
    ) * queries.shape[2] ** (-0.5)
    allowed = (segment[:, None] == segment[None, :]) & (position[None, :] <= position[:, None])
    allowed = allowed & (
        (position[:, None] - position[None, :] < WINDOW) | (position[None, :] < SINK)
    )
    scores = jnp.where(allowed[None, None], scores, -jnp.inf)
    highest = jnp.max(scores, axis=-1, keepdims=True)
    weights_raw = jnp.exp(scores - highest)
    weights = (weights_raw / jnp.sum(weights_raw, axis=-1, keepdims=True)).astype(jnp.bfloat16)
    blended = jnp.einsum("kgqs,skd->qkgd", weights, value_rows, preferred_element_type=jnp.float32)
    return blended.reshape(token_count, -1).astype(jnp.bfloat16)


def spread_rows(first_part, second_part):
    return (
        lax.all_gather(first_part, "mp", axis=0, tiled=True),
        lax.all_gather(second_part, "mp", axis=0, tiled=True),
    )


def sum_rows(term_fn, row_count):
    return lax.psum_scatter(
        term_fn(jnp.int32(0), lax.axis_size("mp") * row_count).astype(jnp.bfloat16),
        "mp",
        scatter_dimension=0,
        tiled=True,
    ).astype(jnp.float32)


def feed_forward(
    residual_stream,
    adapter_indicator,
    feed_norm_gain,
    adapter_down_gate_up,
    adapter_up_gate_up,
    gate_up_full,
    down_full,
    adapter_down_feed,
    adapter_up_feed,
):
    adapter_column_count = adapter_indicator.shape[1]
    model_width = residual_stream.shape[1]
    feed_input = normalize(residual_stream, feed_norm_gain)
    gate_terms = (
        jnp.dot(feed_input, adapter_down_gate_up, preferred_element_type=jnp.float32)
        * jnp.tile(adapter_indicator, (1, 2))
    ).astype(jnp.bfloat16)
    mlp_all, gate_adapter_ranks = spread_rows(feed_input, gate_terms)
    gate_activation = jnp.dot(
        mlp_all, gate_up_full[0], preferred_element_type=jnp.float32
    ) + jnp.dot(
        gate_adapter_ranks[:, :adapter_column_count],
        adapter_up_gate_up[0],
        preferred_element_type=jnp.float32,
    )
    up_projected = jnp.dot(mlp_all, gate_up_full[1], preferred_element_type=jnp.float32) + jnp.dot(
        gate_adapter_ranks[:, adapter_column_count:],
        adapter_up_gate_up[1],
        preferred_element_type=jnp.float32,
    )
    hidden_activation = (jax.nn.silu(gate_activation) * up_projected).astype(jnp.bfloat16)

    def down_term(first_row, row_count):
        projected_rows = lax.dot_general(
            hidden_activation,
            down_full,
            (((1,), (1,)), ((), ())),
            preferred_element_type=jnp.float32,
        )
        return jnp.concatenate(
            [
                projected_rows,
                jnp.dot(hidden_activation, adapter_down_feed, preferred_element_type=jnp.float32),
            ],
            axis=1,
        )

    summed = sum_rows(down_term, residual_stream.shape[0])
    down_adapter_ranks = (summed[:, model_width:] * adapter_indicator).astype(jnp.bfloat16)
    return (
        residual_stream.astype(jnp.float32)
        + summed[:, :model_width]
        + jnp.dot(down_adapter_ranks, adapter_up_feed, preferred_element_type=jnp.float32)
    )


def shards(
    states,
    lengths,
    request_adapters,
    attention_norm_gain,
    query_weight,
    key_weight,
    value_weight,
    output_weight,
    adapter_down_attention,
    adapter_up_query,
    adapter_up_key_value,
    adapter_down_output,
    adapter_up_output,
    feed_norm_gain,
    gate_up_weight,
    down_weight,
    adapter_down_gate_up,
    adapter_up_gate_up,
    adapter_down_feed,
    adapter_up_feed,
):
    mp_count = lax.axis_size("mp")
    group_index = lax.axis_index("req")
    mp_index = lax.axis_index("mp")
    slot_dev = states.shape[1]
    model_width = states.shape[3]
    adapter_column_count = adapter_up_output.shape[0]
    total_rows = slot_dev * mp_count
    gate_up_full, down_full = (
        lax.all_gather(gate_up_weight, "req", axis=1, tiled=True),
        lax.all_gather(down_weight, "req", axis=0, tiled=True),
    )
    local_rows = states.reshape(slot_dev, model_width)
    own_lengths = lax.dynamic_index_in_dim(lengths, group_index, 0, keepdims=False)
    own_adapters = lax.dynamic_index_in_dim(request_adapters, group_index, 0, keepdims=False)
    request_count = own_lengths.shape[0]
    local_slots = jnp.arange(slot_dev, dtype=jnp.int32) * mp_count + mp_index
    living, unused_pos, unused_seg, adapter_within = slot_info(
        jnp.broadcast_to(own_lengths[None, :], (slot_dev, request_count)),
        jnp.broadcast_to(own_adapters[None, :], (slot_dev, request_count)),
        local_slots,
    )
    indicator_within = adapter_select_mask(adapter_within, adapter_column_count, ADAPTER_RANK)
    normed_rows = normalize(local_rows, attention_norm_gain)
    down_adapter_terms = (
        jnp.dot(normed_rows, adapter_down_attention, preferred_element_type=jnp.float32)
        * jnp.tile(indicator_within, (1, 3))
    ).astype(jnp.bfloat16)
    normed_all, adapter_terms_all = spread_rows(normed_rows, down_adapter_terms)
    gathered = jnp.arange(total_rows, dtype=jnp.int32)
    gathered_slots = gathered % slot_dev * mp_count + gathered // slot_dev
    ignored, position_all, segment_all, unused = slot_info(
        jnp.broadcast_to(own_lengths[None, :], (total_rows, request_count)),
        jnp.broadcast_to(own_adapters[None, :], (total_rows, request_count)),
        gathered_slots,
    )
    query_projected = jnp.dot(
        normed_all, query_weight, preferred_element_type=jnp.float32
    ) + jnp.dot(
        adapter_terms_all[:, :adapter_column_count],
        adapter_up_query,
        preferred_element_type=jnp.float32,
    )
    key_projected = jnp.dot(normed_all, key_weight, preferred_element_type=jnp.float32) + jnp.dot(
        adapter_terms_all[:, adapter_column_count : 2 * adapter_column_count],
        adapter_up_key_value[0],
        preferred_element_type=jnp.float32,
    )
    value_projected = jnp.dot(
        normed_all, value_weight, preferred_element_type=jnp.float32
    ) + jnp.dot(
        adapter_terms_all[:, 2 * adapter_column_count :],
        adapter_up_key_value[1],
        preferred_element_type=jnp.float32,
    )
    kv_pair = jnp.stack([key_projected, value_projected])
    partner = from_partner(kv_pair.astype(jnp.bfloat16), "mp", 0).astype(kv_pair.dtype)
    parity = mp_index % 2
    joined = jnp.where(
        parity == 0,
        jnp.concatenate([kv_pair, partner], axis=2),
        jnp.concatenate([partner, kv_pair], axis=2),
    )
    key_projected = joined[0]
    value_projected = joined[1]
    queries = rotate(query_projected.reshape(total_rows, -1, HEAD_SIZE), position_all).astype(
        jnp.bfloat16
    )
    key_rows = rotate(key_projected.reshape(total_rows, -1, HEAD_SIZE), position_all).astype(
        jnp.bfloat16
    )
    value_rows = value_projected.reshape(total_rows, -1, HEAD_SIZE).astype(jnp.bfloat16)
    attention_output = attend(queries, key_rows, value_rows, position_all, segment_all)

    def out_term(first_row, row_count):
        return jnp.concatenate(
            [
                jnp.dot(attention_output, output_weight, preferred_element_type=jnp.float32),
                jnp.dot(attention_output, adapter_down_output, preferred_element_type=jnp.float32),
            ],
            axis=1,
        )

    summed = sum_rows(out_term, slot_dev)
    output_adapter_ranks = (summed[:, model_width:] * indicator_within).astype(jnp.bfloat16)
    residual_stream = (
        local_rows.astype(jnp.float32)
        + summed[:, :model_width]
        + jnp.dot(output_adapter_ranks, adapter_up_output, preferred_element_type=jnp.float32)
    ).astype(jnp.bfloat16)
    layer_result = feed_forward(
        residual_stream,
        indicator_within,
        feed_norm_gain,
        adapter_down_gate_up,
        adapter_up_gate_up,
        gate_up_full,
        down_full,
        adapter_down_feed,
        adapter_up_feed,
    )
    finished = jnp.where(living[:, None], layer_result, jnp.zeros_like(layer_result)).astype(
        jnp.bfloat16
    )
    return finished.reshape(1, slot_dev, 1, model_width)


def solution(mesh):
    placed = (
        P("req", None, "mp", None),
        P(),
        P(),
        P(),
        P(None, "mp"),
        P(None, "mp"),
        P(None, "mp"),
        P("mp", None),
        P(),
        P(None, "mp"),
        P(None, None, "mp"),
        P("mp", None),
        P(),
        P(),
        P(None, "req", "mp"),
        P("req", "mp"),
        P(),
        P(None, None, "mp"),
        P("mp", None),
        P(),
    )
    return jax.shard_map(
        shards, mesh=mesh, in_specs=placed, out_specs=P("req", None, "mp", None), check_vma=False
    )
```

profile of v0, /device:TPU:0, one launch (start us, length us, event | category | flops | bytes accessed | tf_op | source)
XLA Modules:
  0.0 374.3 jit_solution(9356517427873892993)
XLA Ops:
  7.4 1.3 fusion.17
  8.7 1.9 fusion.19
  10.6 0.9 dynamic-slice_reduce_fusion
  12.3 2.9 fusion.12
  15.2 25.0 %all_gather.19 = bf16[512,384]{1,0:T(8,128)(2,1)S(1)} all-gather(bf16[32,384]{1,0:T(8,128)(2,1)S(1)} %fusion.12), channel_id=1, replica_groups=mesh['req'=8,'mp'=16] {'mp'}, dimensions={0}, use_global_device_ids=true | all-gather | bytes 417792 | tf_op jit(solution)/shard_map/all_gather | solution.py:86
  40.4 1.2 fusion.16
  41.6 1.8 multiply_cosine_fusion
  43.4 26.8 %all-gather.5.cloned.1.call-done = bf16[512,5120]{1,0:T(8,128)(2,1)} async-done(((bf16[32,5120]{1,0:T(8,128)(2,1)}), bf16[512,5120]{1,0:T(8,128)(2,1)}) %all-gather.5.cloned.1.call-update) | async-done | bytes 5242896 | tf_op jit(solution)/shard_map/all_gather | solution.py:85
  70.2 4.5 %fusion.76 = f32[512,64]{0,1:T(8,128)S(1)} fusion(bf16[512,5120]{1,0:T(8,128)(2,1)} %all-gather.5.cloned.1.call-done, bf16[5120,64]{0,1:T(8,128)(2,1)} %param.26), kind=kOutput, calls=%fused_computation.140 | convolution fusion | flops 335544320 | bytes 6029312 | tf_op jit(solution)/shard_map/dot_general | solution.py:225
  74.9 1.7 fusion.75
  77.5 1.4 collective-permute-start
  78.9 1.6 fusion.77
  81.6 1.1 copy.44
  82.7 1.9 copy.45
  84.7 1.4 subtract_convert_fusion
  88.3 1.6 convolution_convert_fusion
  90.1 2.7 pad_maximum_fusion
  93.7 78.0 %reduce-scatter.3.cloned.1.call-done = bf16[32,5248]{1,0:T(8,128)(2,1)} async-done(((bf16[512,5248]{1,0:T(8,128)(2,1)}), bf16[32,5248]{1,0:T(8,128)(2,1)}) %reduce-scatter.3.cloned.1.call-update) | async-done | bytes 335888 | tf_op jit(solution)/shard_map/reduce_scatter | solution.py:91
  171.7 1.0 convert_element_type.118
  173.3 0.9 multiply_convert_fusion
  174.8 2.4 fusion.13
  177.2 23.4 %all_gather.22 = bf16[512,256]{1,0:T(8,128)(2,1)S(1)} all-gather(bf16[32,256]{1,0:T(8,128)(2,1)S(1)} %fusion.13), channel_id=1, replica_groups=mesh['req'=8,'mp'=16] {'mp'}, dimensions={0}, use_global_device_ids=true | all-gather | bytes 278528 | tf_op jit(solution)/shard_map/all_gather | solution.py:86
  200.7 29.8 %all-gather.7.cloned.1.call-done = bf16[512,5120]{1,0:T(8,128)(2,1)} async-done(((bf16[32,5120]{1,0:T(8,128)(2,1)}), bf16[512,5120]{1,0:T(8,128)(2,1)}) %all-gather.7.cloned.1.call-update) | async-done | bytes 5242896 | tf_op jit(solution)/shard_map/all_gather | solution.py:85
  230.5 8.7 %fusion.1 = f32[512,640]{1,0:T(8,128)S(1)} fusion(bf16[512,5120]{1,0:T(8,128)(2,1)} %all-gather.7.cloned.1.call-done, bf16[2,5120,640]{2,1,0:T(8,128)(2,1)} %all-gather.9.cloned.1.call-done), kind=kOutput, calls=%fused_computation.5 | convolution fusion | flops 3355443200 | bytes 13107200 | tf_op jit(solution)/shard_map/dot_general | solution.py:118
  239.2 1.2 convolution_add_fusion.3
  240.5 4.3 %fusion = f32[512,640]{1,0:T(8,128)S(1)} fusion(bf16[512,5120]{1,0:T(8,128)(2,1)S(1)} %copy-done.24, bf16[2,5120,640]{2,1,0:T(8,128)(2,1)S(1)} %copy-done.23), kind=kOutput, calls=%fused_computation.3 | convolution fusion | flops 3355443200 | bytes 13107200 | tf_op jit(solution)/shard_map/dot_general | solution.py:125
  246.0 27.8 %all-gather.11.cloned.1.call-done = bf16[5120,640]{1,0:T(8,128)(2,1)} async-done(((bf16[640,640]{1,0:T(8,128)(2,1)}), bf16[5120,640]{1,0:T(8,128)(2,1)}) %all-gather.11.cloned.1.call-update) | async-done | bytes 6553616 | tf_op jit(solution)/shard_map/all_gather | solution.py:187
  273.9 7.3 %convolution_convert_fusion.1 = bf16[512,5120]{1,0:T(8,128)(2,1)S(1)} fusion(bf16[512,640]{1,0:T(8,128)(2,1)S(1)} %fusion.9, bf16[5120,640]{1,0:T(8,128)(2,1)} %all-gather.11.cloned.1.call-done), kind=kOutput, calls=%fused_computation.1 | convolution fusion | flops 3358064640 | bytes 12451840 | tf_op jit(solution)/shard_map/dot_general | solution.py:133
  281.2 2.7 pad_maximum_fusion.1
  284.6 79.0 %reduce-scatter.5.cloned.1.call-done = bf16[32,5248]{1,0:T(8,128)(2,1)} async-done(((bf16[512,5248]{1,0:T(8,128)(2,1)}), bf16[32,5248]{1,0:T(8,128)(2,1)}) %reduce-scatter.5.cloned.1.call-update) | async-done | bytes 335888 | tf_op jit(solution)/shard_map/reduce_scatter | solution.py:91
  363.5 1.0 convert_element_type.125
  364.5 2.4 fusion.6
  (103 shorter events, 9.3 us)
Async XLA Ops:
  7.4 80.9 %copy-start = (bf16[256,5120]{1,0:T(8,128)(2,1)S(1)}, bf16[256,5120]{1,0:T(8,128)(2,1)}, u32[]{:S(2)}) copy-start(bf16[256,5120]{1,0:T(8,128)(2,1)} %param.27) | copy-start | bytes 7864324
  7.4 62.8 %all-gather.5.cloned.1.call-start = ((), (), s32[]{:S(2)}) async-start(), calls=%async_computation.2 | async-start | bytes 5570560 | tf_op jit(solution)/shard_map/all_gather | solution.py:85
  10.6 161.2 %reduce-scatter.3.cloned.1.call-start = ((), (), s32[]{:S(2)}) async-start(), calls=%async_computation.3 | async-start | bytes 5709824 | tf_op jit(solution)/shard_map/reduce_scatter | solution.py:91
  11.8 31.6 %copy-start.15 = (s32[128]{0:T(128)}, s32[128]{0:T(128)S(1)}, u32[]{:S(2)}) copy-start(s32[128]{0:T(128)S(1)} %and_select_fusion) | copy-start | bytes 1540
  11.9 31.5 %copy-start.17 = (s32[32]{0:T(128)}, s32[32]{0:T(128)S(1)}, u32[]{:S(2)}) copy-start(s32[32]{0:T(128)S(1)} %broadcast_select_fusion) | copy-start | bytes 388
  40.3 3.1 copy-start.19
  40.4 3.0 copy-start.13
  43.4 31.3 %copy-start.11 = (bf16[2,128,64]{1,2,0:T(8,128)(2,1)S(1)}, bf16[2,128,64]{1,2,0:T(8,128)(2,1)}, u32[]{:S(2)}) copy-start(bf16[2,128,64]{1,2,0:T(8,128)(2,1)} %param.30) | copy-start | bytes 98308
  70.2 4.7 %copy-start.2 = (bf16[512,5120]{1,0:T(8,128)(2,1)S(1)}, bf16[512,5120]{1,0:T(8,128)(2,1)}, u32[]{:S(2)}) copy-start(bf16[512,5120]{1,0:T(8,128)(2,1)} %all-gather.5.cloned.1.call-done) | copy-start | bytes 15728644
  70.2 4.7 %copy-start.5 = (bf16[5120,64]{0,1:T(8,128)(2,1)S(1)}, bf16[5120,64]{0,1:T(8,128)(2,1)}, u32[]{:S(2)}) copy-start(bf16[5120,64]{0,1:T(8,128)(2,1)} %param.25) | copy-start | bytes 1966084
  74.9 4.0 %copy-start.25 = (bf16[5120,256]{1,0:T(8,128)(2,1)S(1)}, bf16[5120,256]{1,0:T(8,128)(2,1)}, u32[]{:S(2)}) copy-start(bf16[5120,256]{1,0:T(8,128)(2,1)} %param.24) | copy-start | bytes 7864324
  77.5 3.0 copy-start.9
  77.5 8.6 %collective-permute-start = (bf16[2,512,64]{1,2,0:T(8,128)(2,1)}, bf16[2,512,64]{1,2,0:T(8,128)(2,1)S(1)}, u32[]{:S(2)}, u32[]{:S(2)}) collective-permute-start(bf16[2,512,64]{1,2,0:T(8,128)(2,1)} %maximum_convert_fusion), channel_id=1, source_target_pairs={{0,1},{1,0},{2,3},{3,2},{4,5},{5,4},{6,7},{7,6},{8,9},{9,8},{10,11... | collective-permute-start | bytes 393224 | tf_op jit(solution)/shard_map/ppermute | solution.py:15
  84.7 1.5 copy-start.14
  84.7 1.5 copy-start.20
  84.7 2.1 copy-start.6
  88.3 1.6 copy-start.10
  92.8 79.9 %copy-start.3 = (bf16[1,32,1,5120]{3,1,2,0:T(8,128)(2,1)S(1)}, bf16[1,32,1,5120]{3,1,2,0:T(8,128)(2,1)}, u32[]{:S(2)}) copy-start(bf16[1,32,1,5120]{3,1,2,0:T(8,128)(2,1)} %param.20) | copy-start | bytes 983044
  92.8 79.9 %copy-start.4 = (bf16[128,5120]{1,0:T(8,128)(2,1)S(1)}, bf16[128,5120]{1,0:T(8,128)(2,1)}, u32[]{:S(2)}) copy-start(bf16[128,5120]{1,0:T(8,128)(2,1)} %param.32) | copy-start | bytes 3932164
  92.9 79.9 %copy-start.16 = (s32[128]{0:T(128)S(1)}, s32[128]{0:T(128)}, u32[]{:S(2)}) copy-start(s32[128]{0:T(128)} %copy-done.15) | copy-start | bytes 1540
  92.9 79.9 %copy-start.18 = (s32[32]{0:T(128)S(1)}, s32[32]{0:T(128)}, u32[]{:S(2)}) copy-start(s32[32]{0:T(128)} %copy-done.17) | copy-start | bytes 388
  92.9 80.4 %copy-start.12 = (f32[5120]{0:T(1024)S(1)}, f32[5120]{0:T(1024)}, u32[]{:S(2)}) copy-start(f32[5120]{0:T(1024)} %param.33) | copy-start | bytes 61444
  92.9 107.8 %all-gather.9.cloned.1.call-start = ((), (), s32[]{:S(2)}) async-start(), calls=%async_computation.5 | async-start | bytes 14745600 | tf_op jit(solution)/shard_map/all_gather | solution.py:186
  93.5 137.0 %all-gather.7.cloned.1.call-start = ((), (), s32[]{:S(2)}) async-start(), calls=%async_computation.4 | async-start | bytes 5570560 | tf_op jit(solution)/shard_map/all_gather | solution.py:85
  174.2 99.7 %all-gather.11.cloned.1.call-start = ((), (), s32[]{:S(2)}) async-start(), calls=%async_computation.6 | async-start | bytes 7372800 | tf_op jit(solution)/shard_map/all_gather | solution.py:187
  174.7 188.8 %reduce-scatter.5.cloned.1.call-start = ((), (), s32[]{:S(2)}) async-start(), calls=%async_computation.7 | async-start | bytes 5709824 | tf_op jit(solution)/shard_map/reduce_scatter | solution.py:91
  230.5 10.0 %copy-start.23 = (bf16[2,5120,640]{2,1,0:T(8,128)(2,1)S(1)}, bf16[2,5120,640]{2,1,0:T(8,128)(2,1)}, u32[]{:S(2)}) copy-start(bf16[2,5120,640]{2,1,0:T(8,128)(2,1)} %all-gather.9.cloned.1.call-done) | copy-start | bytes 39321604
  230.5 10.0 %copy-start.24 = (bf16[512,5120]{1,0:T(8,128)(2,1)S(1)}, bf16[512,5120]{1,0:T(8,128)(2,1)}, u32[]{:S(2)}) copy-start(bf16[512,5120]{1,0:T(8,128)(2,1)} %all-gather.7.cloned.1.call-done) | copy-start | bytes 15728644
  240.5 4.3 %copy-start.8 = (bf16[2,128,640]{2,1,0:T(8,128)(2,1)S(1)}, bf16[2,128,640]{2,1,0:T(8,128)(2,1)}, u32[]{:S(2)}) copy-start(bf16[2,128,640]{2,1,0:T(8,128)(2,1)} %param.37) | copy-start | bytes 983044
  244.8 0.9 copy-start.7
  283.9 0.6 copy-start.22
  284.5 82.4 %copy-start.1 = (bf16[256,5120]{1,0:T(8,128)(2,1)S(1)}, bf16[256,5120]{1,0:T(8,128)(2,1)}, u32[]{:S(2)}) copy-start(bf16[256,5120]{1,0:T(8,128)(2,1)} %param.27) | copy-start | bytes 7864324
  (1 other events, 0.5 us)
Sparse Core Ops, SparseCore 0:
  10.7 59.4 all-gather.4
  93.0 78.7 reduce-scatter.2
  284.1 79.3 reduce-scatter.4
Sparse Core Ops, SparseCore 1:
  95.1 69.0 all-gather.8
  174.2 56.2 all-gather.6
  232.0 41.8 all-gather.10
where the time goes:
time: 375 us; the launch traced here: 374 us
  waiting for transfers between devices  243 us (65%)
  blocking collectives  48.4 us (13%)
  matrix products  41.9 us (11%)
  other arithmetic  17.8 us (5%)
  between operations  15.3 us (4%)
  local copies, waits for them, and re-layouts  6.46 us (2%)
    reduce_scatter x2, waiting for transfers between devices, sum_rows(): lax.psum_scatter(term_fn(jnp.int32(0), lax.axis_size('mp') * row_count).a...  157 us
    all_gather x2, waiting for transfers between devices, spread_rows(): lax.all_gather(first_part, 'mp', axis=0, tiled=True)  56.6 us
    all_gather x2, blocking collectives, spread_rows(): lax.all_gather(second_part, 'mp', axis=0, tiled=True)  48.4 us
    all_gather x1, waiting for transfers between devices, shards(): lax.all_gather(down_weight, 'req', axis=0, tiled=True)  27.8 us
    dot_general x1, matrix products, feed_forward(): jnp.dot(mlp_all, gate_up_full[0], preferred_element_type=jnp.float32)  8.72 us
  transfers between devices with their start and end apart: 7, of which 5 were waited for; matrix products, arithmetic and copies ran while one was open for 9% of the time, Pallas kernels for 0%

commit v1 on v0

--- a/solution.py
+++ b/solution.py
@@ -9,6 +9,19 @@
 SINK = 4
 EPSILON = 1e-05
 ROPE_THETA = 1000000.0
+
+
+def gather_around(value, axis, dim):
+    ways = lax.axis_size(axis)
+    up = [(d, (d + 1) % ways) for d in range(ways)]
+    down = [(d, (d - 1) % ways) for d in range(ways)]
+    earlier, later = ([value], [value])
+    for _ in range(ways // 2):
+        earlier.append(lax.ppermute(earlier[-1], axis, up))
+    for _ in range((ways - 1) // 2):
+        later.append(lax.ppermute(later[-1], axis, down))
+    line = jnp.concatenate([*earlier[::-1], *later[1:]], axis=dim)
+    return jnp.roll(line, (lax.axis_index(axis) - ways // 2) * value.shape[dim], axis=dim)
 
 
 def from_partner(shard, axis, stride):
@@ -82,7 +95,7 @@
 
 def spread_rows(first_part, second_part):
     return (
-        lax.all_gather(first_part, "mp", axis=0, tiled=True),
+        gather_around(first_part, "mp", 0),
         lax.all_gather(second_part, "mp", axis=0, tiled=True),
     )
 

time: 375 us -> 483 us (1.29); the launches traced: 374 us -> 475 us
  starting transfers between devices: 1.82 us -> 74.3 us
  local copies, waits for them, and re-layouts: 6.46 us -> 29.9 us
  waiting for transfers between devices: 243 us -> 233 us
  other arithmetic: 17.8 us -> 23.7 us
    ppermute x0 -> x30, waiting for transfers between devices: none -> 78.2 us  [the longest x16 64 us: gather_around(): earlier.append(lax.ppermute(earlier[-1], axis, up))]
    ppermute x0 -> x30, starting transfers between devices: none -> 74 us  [the longest x14 70.2 us: gather_around(): later.append(lax.ppermute(later[-1], axis, down))]
    all_gather x2 -> x0, waiting for transfers between devices: 56.6 us -> none  [spread_rows(): lax.all_gather(first_part, 'mp', axis=0, tiled=True)]
    all_gather x1, waiting for transfers between devices: 27.8 us -> 0.03 us  [shards(): lax.all_gather(down_weight, 'req', axis=0, tiled=True)]
    unnamed x54 -> x126, local copies, waits for them, and re-layouts: 4.53 us -> 27.2 us
    concatenate x0 -> x1, other arithmetic: none -> 4.88 us  [gather_around(): jnp.roll(line, (lax.axis_index(axis) - ways // 2) * value.shape[dim], axi...]
  transfers between devices with their start and end apart: 7 -> 35, of which waited for: 5 -> 17; matrix products, arithmetic and copies ran while one was open for 9% -> 14% of each run, Pallas kernels for 0% -> 0%
where the time goes in v1:
time: 483 us; the launch traced here: 475 us
  waiting for transfers between devices  233 us (48%)
  starting transfers between devices  74.3 us (15%)
  blocking collectives  52.6 us (11%)
  matrix products  46 us (10%)
  local copies, waits for them, and re-layouts  29.9 us (6%)
  other arithmetic  23.7 us (5%)
  between operations  15.9 us (3%)
    reduce_scatter x2, waiting for transfers between devices, sum_rows(): lax.psum_scatter(term_fn(jnp.int32(0), lax.axis_size('mp') * row_count).a...  154 us
    ppermute x14, starting transfers between devices, gather_around(): later.append(lax.ppermute(later[-1], axis, down))  70.2 us
    ppermute x16, waiting for transfers between devices, gather_around(): earlier.append(lax.ppermute(earlier[-1], axis, up))  64 us
    all_gather x2, blocking collectives, spread_rows(): lax.all_gather(second_part, 'mp', axis=0, tiled=True)  52.6 us
    unnamed x126, local copies, waits for them, and re-layouts  27.2 us
    ppermute x14, waiting for transfers between devices, gather_around(): later.append(lax.ppermute(later[-1], axis, down))  14.2 us
  transfers between devices with their start and end apart: 35, of which 17 were waited for; matrix products, arithmetic and copies ran while one was open for 14% of the time, Pallas kernels for 0%

profile of v1, /device:TPU:0, one launch (start us, length us, event | category | flops | bytes accessed | tf_op | source)
XLA Modules:
  0.0 475.4 jit_solution(12769355649864329331)
XLA Ops:
  11.6 3.7 collective-permute-start.8
  16.6 6.3 %collective-permute-done = bf16[32,5120]{1,0:T(8,128)(2,1)S(1)} collective-permute-done((bf16[32,5120]{1,0:T(8,128)(2,1)S(1)}, bf16[32,5120]{1,0:T(8,128)(2,1)S(1)}, u32[]{:S(2)}, u32[]{:S(2)}) %collective-permute-start) | collective-permute-done | bytes 327712 | tf_op jit(solution)/shard_map/ppermute | solution.py:20
  23.0 12.1 %collective-permute-done.1 = bf16[32,5120]{1,0:T(8,128)(2,1)S(1)} collective-permute-done((bf16[32,5120]{1,0:T(8,128)(2,1)S(1)}, bf16[32,5120]{1,0:T(8,128)(2,1)S(1)}, u32[]{:S(2)}, u32[]{:S(2)}) %collective-permute-start.1) | collective-permute-done | bytes 327712 | tf_op jit(solution)/shard_map/ppermute | solution.py:20
  35.1 5.4 %collective-permute-start.9 = (bf16[32,5120]{1,0:T(8,128)(2,1)}, bf16[32,5120]{1,0:T(8,128)(2,1)S(1)}, u32[]{:S(2)}, u32[]{:S(2)}) collective-permute-start(bf16[32,5120]{1,0:T(8,128)(2,1)} %collective-permute-done.8), channel_id=1, source_target_pairs={{0,15},{1,0},{2,1},{3,2},{4,3},{5,4},{6,5},{7,6},{8,7},{9,8},{10,9... | collective-permute-start | bytes 983048 | tf_op jit(solution)/shard_map/ppermute | solution.py:22
  40.5 5.8 %collective-permute-done.2 = bf16[32,5120]{1,0:T(8,128)(2,1)S(1)} collective-permute-done((bf16[32,5120]{1,0:T(8,128)(2,1)S(1)}, bf16[32,5120]{1,0:T(8,128)(2,1)S(1)}, u32[]{:S(2)}, u32[]{:S(2)}) %collective-permute-start.2) | collective-permute-done | bytes 327712 | tf_op jit(solution)/shard_map/ppermute | solution.py:20
  49.3 5.3 %collective-permute-start.10 = (bf16[32,5120]{1,0:T(8,128)(2,1)S(1)}, bf16[32,5120]{1,0:T(8,128)(2,1)S(1)}, u32[]{:S(2)}, u32[]{:S(2)}) collective-permute-start(bf16[32,5120]{1,0:T(8,128)(2,1)S(1)} %collective-permute-done.9), channel_id=1, source_target_pairs={{0,15},{1,0},{2,1},{3,2},{4,3},{5,4},{6,5},{7,6},{8,7},{9,8},{10,9... | collective-permute-start | bytes 983048 | tf_op jit(solution)/shard_map/ppermute | solution.py:22
  56.7 25.8 %all_gather.12 = bf16[512,384]{1,0:T(8,128)(2,1)S(1)} all-gather(bf16[32,384]{1,0:T(8,128)(2,1)S(1)} %fusion.14), channel_id=1, replica_groups=mesh['req'=8,'mp'=16] {'mp'}, dimensions={0}, use_global_device_ids=true | all-gather | bytes 417792 | tf_op jit(solution)/shard_map/all_gather | solution.py:99
  82.7 4.6 collective-permute-start.11
  88.2 5.6 %collective-permute-done.11 = bf16[32,5120]{1,0:T(8,128)(2,1)S(1)} collective-permute-done((bf16[32,5120]{1,0:T(8,128)(2,1)S(1)}, bf16[32,5120]{1,0:T(8,128)(2,1)S(1)}, u32[]{:S(2)}, u32[]{:S(2)}) %collective-permute-start.11) | collective-permute-done | bytes 327712 | tf_op jit(solution)/shard_map/ppermute | solution.py:22
  93.8 5.8 %collective-permute-start.12 = (bf16[32,5120]{1,0:T(8,128)(2,1)S(1)}, bf16[32,5120]{1,0:T(8,128)(2,1)}, u32[]{:S(2)}, u32[]{:S(2)}) collective-permute-start(bf16[32,5120]{1,0:T(8,128)(2,1)S(1)} %collective-permute-done.11), channel_id=1, source_target_pairs={{0,15},{1,0},{2,1},{3,2},{4,3},{5,4},{6,5},{7,6},{8,7},{9,8},{10,9... | collective-permute-start | bytes 983048 | tf_op jit(solution)/shard_map/ppermute | solution.py:22
  101.6 3.9 collective-permute-done.12
  105.5 5.9 %collective-permute-start.13 = (bf16[32,5120]{1,0:T(8,128)(2,1)}, bf16[32,5120]{1,0:T(8,128)(2,1)}, u32[]{:S(2)}, u32[]{:S(2)}) collective-permute-start(bf16[32,5120]{1,0:T(8,128)(2,1)} %collective-permute-done.12), channel_id=1, source_target_pairs={{0,15},{1,0},{2,1},{3,2},{4,3},{5,4},{6,5},{7,6},{8,7},{9,8},{10,9... | collective-permute-start | bytes 983048 | tf_op jit(solution)/shard_map/ppermute | solution.py:22
  117.0 6.2 %collective-permute-start.14 = (bf16[32,5120]{1,0:T(8,128)(2,1)}, bf16[32,5120]{1,0:T(8,128)(2,1)S(1)}, u32[]{:S(2)}, u32[]{:S(2)}) collective-permute-start(bf16[32,5120]{1,0:T(8,128)(2,1)} %collective-permute-done.13), channel_id=1, source_target_pairs={{0,15},{1,0},{2,1},{3,2},{4,3},{5,4},{6,5},{7,6},{8,7},{9,8},{10,9... | collective-permute-start | bytes 983048 | tf_op jit(solution)/shard_map/ppermute | solution.py:22
  134.2 4.9 %fusion.8 = bf16[512,5120]{1,0:T(8,128)(2,1)S(1)} fusion(s32[]{:T(128)S(6)} %select_n.173, bf16[512,5120]{1,0:T(8,128)(2,1)S(1)} %constant_dynamic-update-slice_fusion), kind=kLoop, calls=%fused_computation.20 | loop fusion | flops 10485760 | bytes 10485764 | tf_op jit(solution)/shard_map/jit(_roll_dynamic)/concatenate | solution.py:24
  159.6 77.4 %reduce-scatter.3.cloned.1.call-done = bf16[32,5248]{1,0:T(8,128)(2,1)} async-done(((bf16[512,5248]{1,0:T(8,128)(2,1)}), bf16[32,5248]{1,0:T(8,128)(2,1)}) %reduce-scatter.3.cloned.1.call-update) | async-done | bytes 335888 | tf_op jit(solution)/shard_map/reduce_scatter | solution.py:104
  239.9 10.5 %collective-permute-done.16 = bf16[32,5120]{1,0:T(8,128)(2,1)S(1)} collective-permute-done((bf16[32,5120]{1,0:T(8,128)(2,1)S(1)}, bf16[32,5120]{1,0:T(8,128)(2,1)S(1)}, u32[]{:S(2)}, u32[]{:S(2)}) %collective-permute-start.16) | collective-permute-done | bytes 327712 | tf_op jit(solution)/shard_map/ppermute | solution.py:20
  250.4 5.3 %collective-permute-start.24 = (bf16[32,5120]{1,0:T(8,128)(2,1)S(1)}, bf16[32,5120]{1,0:T(8,128)(2,1)S(1)}, u32[]{:S(2)}, u32[]{:S(2)}) collective-permute-start(bf16[32,5120]{1,0:T(8,128)(2,1)S(1)} %multiply_convert_fusion.1), channel_id=1, source_target_pairs={{0,15},{1,0},{2,1},{3,2},{4,3},{5,4},{6,5},{7,6},{8,7},{9,8},{10,9... | collective-permute-start | bytes 983048 | tf_op jit(solution)/shard_map/ppermute | solution.py:22
  255.7 5.4 %collective-permute-done.17 = bf16[32,5120]{1,0:T(8,128)(2,1)S(1)} collective-permute-done((bf16[32,5120]{1,0:T(8,128)(2,1)S(1)}, bf16[32,5120]{1,0:T(8,128)(2,1)S(1)}, u32[]{:S(2)}, u32[]{:S(2)}) %collective-permute-start.17) | collective-permute-done | bytes 327712 | tf_op jit(solution)/shard_map/ppermute | solution.py:20
  261.1 5.3 %collective-permute-start.25 = (bf16[32,5120]{1,0:T(8,128)(2,1)S(1)}, bf16[32,5120]{1,0:T(8,128)(2,1)S(1)}, u32[]{:S(2)}, u32[]{:S(2)}) collective-permute-start(bf16[32,5120]{1,0:T(8,128)(2,1)S(1)} %collective-permute-done.24), channel_id=1, source_target_pairs={{0,15},{1,0},{2,1},{3,2},{4,3},{5,4},{6,5},{7,6},{8,7},{9,8},{10,9... | collective-permute-start | bytes 983048 | tf_op jit(solution)/shard_map/ppermute | solution.py:22
  266.5 5.0 %collective-permute-done.18 = bf16[32,5120]{1,0:T(8,128)(2,1)S(1)} collective-permute-done((bf16[32,5120]{1,0:T(8,128)(2,1)S(1)}, bf16[32,5120]{1,0:T(8,128)(2,1)S(1)}, u32[]{:S(2)}, u32[]{:S(2)}) %collective-permute-start.18) | collective-permute-done | bytes 327712 | tf_op jit(solution)/shard_map/ppermute | solution.py:20
  271.5 5.3 %collective-permute-start.26 = (bf16[32,5120]{1,0:T(8,128)(2,1)S(1)}, bf16[32,5120]{1,0:T(8,128)(2,1)S(1)}, u32[]{:S(2)}, u32[]{:S(2)}) collective-permute-start(bf16[32,5120]{1,0:T(8,128)(2,1)S(1)} %collective-permute-done.25), channel_id=1, source_target_pairs={{0,15},{1,0},{2,1},{3,2},{4,3},{5,4},{6,5},{7,6},{8,7},{9,8},{10,9... | collective-permute-start | bytes 983048 | tf_op jit(solution)/shard_map/ppermute | solution.py:22
  276.9 5.0 %collective-permute-done.19 = bf16[32,5120]{1,0:T(8,128)(2,1)S(1)} collective-permute-done((bf16[32,5120]{1,0:T(8,128)(2,1)S(1)}, bf16[32,5120]{1,0:T(8,128)(2,1)S(1)}, u32[]{:S(2)}, u32[]{:S(2)}) %collective-permute-start.19) | collective-permute-done | bytes 327712 | tf_op jit(solution)/shard_map/ppermute | solution.py:20
  282.6 4.7 collective-permute-start.27
  287.3 5.3 %collective-permute-done.20 = bf16[32,5120]{1,0:T(8,128)(2,1)} collective-permute-done((bf16[32,5120]{1,0:T(8,128)(2,1)S(1)}, bf16[32,5120]{1,0:T(8,128)(2,1)}, u32[]{:S(2)}, u32[]{:S(2)}) %collective-permute-start.20) | collective-permute-done | bytes 327712 | tf_op jit(solution)/shard_map/ppermute | solution.py:20
  292.8 5.6 %collective-permute-start.28 = (bf16[32,5120]{1,0:T(8,128)(2,1)S(1)}, bf16[32,5120]{1,0:T(8,128)(2,1)S(1)}, u32[]{:S(2)}, u32[]{:S(2)}) collective-permute-start(bf16[32,5120]{1,0:T(8,128)(2,1)S(1)} %collective-permute-done.27), channel_id=1, source_target_pairs={{0,15},{1,0},{2,1},{3,2},{4,3},{5,4},{6,5},{7,6},{8,7},{9,8},{10,9... | collective-permute-start | bytes 983048 | tf_op jit(solution)/shard_map/ppermute | solution.py:22
  298.4 6.3 %collective-permute-done.21 = bf16[32,5120]{1,0:T(8,128)(2,1)} collective-permute-done((bf16[32,5120]{1,0:T(8,128)(2,1)}, bf16[32,5120]{1,0:T(8,128)(2,1)}, u32[]{:S(2)}, u32[]{:S(2)}) %collective-permute-start.21) | collective-permute-done | bytes 327712 | tf_op jit(solution)/shard_map/ppermute | solution.py:20
  307.3 26.8 %all_gather.14 = bf16[512,256]{1,0:T(8,128)(2,1)S(1)} all-gather(bf16[32,256]{1,0:T(8,128)(2,1)S(1)} %fusion.15), channel_id=1, replica_groups=mesh['req'=8,'mp'=16] {'mp'}, dimensions={0}, use_global_device_ids=true | all-gather | bytes 278528 | tf_op jit(solution)/shard_map/all_gather | solution.py:99
  341.7 4.9 %collective-permute-start.30 = (bf16[32,5120]{1,0:T(8,128)(2,1)S(1)}, bf16[32,5120]{1,0:T(8,128)(2,1)S(1)}, u32[]{:S(2)}, u32[]{:S(2)}) collective-permute-start(bf16[32,5120]{1,0:T(8,128)(2,1)S(1)} %collective-permute-done.29), channel_id=1, source_target_pairs={{0,15},{1,0},{2,1},{3,2},{4,3},{5,4},{6,5},{7,6},{8,7},{9,8},{10,9... | collective-permute-start | bytes 983048 | tf_op jit(solution)/shard_map/ppermute | solution.py:22
  360.8 8.3 %fusion.10 = f32[512,640]{1,0:T(8,128)S(1)} fusion(f32[512,640]{1,0:T(8,128)S(1)} %fusion.31, bf16[2,5120,640]{2,1,0:T(8,128)(2,1)} %all-gather.3.cloned.1.call-done, s32[]{:T(128)S(6)} %select_n.173, bf16[512,5120]{1,0:T(8,128)(2,1)} %constant_dynamic-update-slice_fusion.16), kind=kOutput, calls=%fused_computation.25 | convolution fusion | flops 3366256640 | bytes 14417924 | tf_op jit(solution)/shard_map/dot_general | solution.py:131
  369.1 7.1 %multiply_convert_fusion = bf16[512,640]{1,0:T(8,128)(2,1)S(1)} fusion(f32[512,640]{1,0:T(8,128)S(1)} %fusion.10, f32[512,640]{1,0:T(8,128)S(1)} %fusion.29, bf16[2,5120,640]{2,1,0:T(8,128)(2,1)S(1)} %copy-done.46, s32[]{:T(128)S(6)} %select_n.173, bf16[512,5120]{1,0:T(8,128)(2,1)} %constant_dynamic-update-slice_fusion.16), kind=kOutput, calls=%fused_computation.27 | convolution fusion | flops 3368222720 | bytes 15073284 | tf_op jit(solution)/shard_map/dot_general | solution.py:138
  376.6 7.4 %convolution_convert_fusion.1 = bf16[512,5120]{1,0:T(8,128)(2,1)S(1)} fusion(bf16[512,640]{1,0:T(8,128)(2,1)S(1)} %multiply_convert_fusion, bf16[5120,640]{1,0:T(8,128)(2,1)} %all-gather.5.cloned.1.call-done), kind=kOutput, calls=%fused_computation.5 | convolution fusion | flops 3358064640 | bytes 12451840 | tf_op jit(solution)/shard_map/dot_general | solution.py:146
  387.4 76.9 %reduce-scatter.5.cloned.1.call-done = bf16[32,5248]{1,0:T(8,128)(2,1)} async-done(((bf16[512,5248]{1,0:T(8,128)(2,1)}), bf16[32,5248]{1,0:T(8,128)(2,1)}) %reduce-scatter.5.cloned.1.call-update) | async-done | bytes 335888 | tf_op jit(solution)/shard_map/reduce_scatter | solution.py:104
  (234 shorter events, 85.5 us)
Async XLA Ops:
  7.4 229.6 %reduce-scatter.3.cloned.1.call-start = ((), (), s32[]{:S(2)}) async-start(), calls=%async_computation.2 | async-start | bytes 5709824 | tf_op jit(solution)/shard_map/reduce_scatter | solution.py:104
  9.8 13.1 %collective-permute-start = (bf16[32,5120]{1,0:T(8,128)(2,1)S(1)}, bf16[32,5120]{1,0:T(8,128)(2,1)S(1)}, u32[]{:S(2)}, u32[]{:S(2)}) collective-permute-start(bf16[32,5120]{1,0:T(8,128)(2,1)S(1)} %fusion.21), channel_id=1, source_target_pairs={{0,1},{1,2},{2,3},{3,4},{4,5},{5,6},{6,7},{7,8},{8,9},{9,10},{10,1... | collective-permute-start | bytes 983048 | tf_op jit(solution)/shard_map/ppermute | solution.py:20
  11.6 23.6 %collective-permute-start.8 = (bf16[32,5120]{1,0:T(8,128)(2,1)S(1)}, bf16[32,5120]{1,0:T(8,128)(2,1)}, u32[]{:S(2)}, u32[]{:S(2)}) collective-permute-start(bf16[32,5120]{1,0:T(8,128)(2,1)S(1)} %fusion.21), channel_id=1, source_target_pairs={{0,15},{1,0},{2,1},{3,2},{4,3},{5,4},{6,5},{7,6},{8,7},{9,8},{10,9... | collective-permute-start | bytes 983048 | tf_op jit(solution)/shard_map/ppermute | solution.py:22
  22.9 12.2 %collective-permute-start.1 = (bf16[32,5120]{1,0:T(8,128)(2,1)S(1)}, bf16[32,5120]{1,0:T(8,128)(2,1)S(1)}, u32[]{:S(2)}, u32[]{:S(2)}) collective-permute-start(bf16[32,5120]{1,0:T(8,128)(2,1)S(1)} %collective-permute-done), channel_id=1, source_target_pairs={{0,1},{1,2},{2,3},{3,4},{4,5},{5,6},{6,7},{7,8},{8,9},{9,10},{10,1... | collective-permute-start | bytes 983048 | tf_op jit(solution)/shard_map/ppermute | solution.py:20
  35.1 11.2 %collective-permute-start.2 = (bf16[32,5120]{1,0:T(8,128)(2,1)S(1)}, bf16[32,5120]{1,0:T(8,128)(2,1)S(1)}, u32[]{:S(2)}, u32[]{:S(2)}) collective-permute-start(bf16[32,5120]{1,0:T(8,128)(2,1)S(1)} %collective-permute-done.1), channel_id=1, source_target_pairs={{0,1},{1,2},{2,3},{3,4},{4,5},{5,6},{6,7},{7,8},{8,9},{9,10},{10,1... | collective-permute-start | bytes 983048 | tf_op jit(solution)/shard_map/ppermute | solution.py:20
  35.1 14.1 %collective-permute-start.9 = (bf16[32,5120]{1,0:T(8,128)(2,1)}, bf16[32,5120]{1,0:T(8,128)(2,1)S(1)}, u32[]{:S(2)}, u32[]{:S(2)}) collective-permute-start(bf16[32,5120]{1,0:T(8,128)(2,1)} %collective-permute-done.8), channel_id=1, source_target_pairs={{0,15},{1,0},{2,1},{3,2},{4,3},{5,4},{6,5},{7,6},{8,7},{9,8},{10,9... | collective-permute-start | bytes 983048 | tf_op jit(solution)/shard_map/ppermute | solution.py:22
  46.3 10.4 %collective-permute-start.3 = (bf16[32,5120]{1,0:T(8,128)(2,1)S(1)}, bf16[32,5120]{1,0:T(8,128)(2,1)S(1)}, u32[]{:S(2)}, u32[]{:S(2)}) collective-permute-start(bf16[32,5120]{1,0:T(8,128)(2,1)S(1)} %collective-permute-done.2), channel_id=1, source_target_pairs={{0,1},{1,2},{2,3},{3,4},{4,5},{5,6},{6,7},{7,8},{8,9},{9,10},{10,1... | collective-permute-start | bytes 983048 | tf_op jit(solution)/shard_map/ppermute | solution.py:20
  49.3 33.4 %collective-permute-start.10 = (bf16[32,5120]{1,0:T(8,128)(2,1)S(1)}, bf16[32,5120]{1,0:T(8,128)(2,1)S(1)}, u32[]{:S(2)}, u32[]{:S(2)}) collective-permute-start(bf16[32,5120]{1,0:T(8,128)(2,1)S(1)} %collective-permute-done.9), channel_id=1, source_target_pairs={{0,15},{1,0},{2,1},{3,2},{4,3},{5,4},{6,5},{7,6},{8,7},{9,8},{10,9... | collective-permute-start | bytes 983048 | tf_op jit(solution)/shard_map/ppermute | solution.py:22
  56.7 30.6 %collective-permute-start.4 = (bf16[32,5120]{1,0:T(8,128)(2,1)S(1)}, bf16[32,5120]{1,0:T(8,128)(2,1)S(1)}, u32[]{:S(2)}, u32[]{:S(2)}) collective-permute-start(bf16[32,5120]{1,0:T(8,128)(2,1)S(1)} %collective-permute-done.3), channel_id=1, source_target_pairs={{0,1},{1,2},{2,3},{3,4},{4,5},{5,6},{6,7},{7,8},{8,9},{9,10},{10,1... | collective-permute-start | bytes 983048 | tf_op jit(solution)/shard_map/ppermute | solution.py:20
  82.7 11.2 %collective-permute-start.11 = (bf16[32,5120]{1,0:T(8,128)(2,1)S(1)}, bf16[32,5120]{1,0:T(8,128)(2,1)S(1)}, u32[]{:S(2)}, u32[]{:S(2)}) collective-permute-start(bf16[32,5120]{1,0:T(8,128)(2,1)S(1)} %collective-permute-done.10), channel_id=1, source_target_pairs={{0,15},{1,0},{2,1},{3,2},{4,3},{5,4},{6,5},{7,6},{8,7},{9,8},{10,9... | collective-permute-start | bytes 983048 | tf_op jit(solution)/shard_map/ppermute | solution.py:22
  87.3 12.3 %collective-permute-start.5 = (bf16[32,5120]{1,0:T(8,128)(2,1)S(1)}, bf16[32,5120]{1,0:T(8,128)(2,1)S(1)}, u32[]{:S(2)}, u32[]{:S(2)}) collective-permute-start(bf16[32,5120]{1,0:T(8,128)(2,1)S(1)} %collective-permute-done.4), channel_id=1, source_target_pairs={{0,1},{1,2},{2,3},{3,4},{4,5},{5,6},{6,7},{7,8},{8,9},{9,10},{10,1... | collective-permute-start | bytes 983048 | tf_op jit(solution)/shard_map/ppermute | solution.py:20
  93.8 11.6 %collective-permute-start.12 = (bf16[32,5120]{1,0:T(8,128)(2,1)S(1)}, bf16[32,5120]{1,0:T(8,128)(2,1)}, u32[]{:S(2)}, u32[]{:S(2)}) collective-permute-start(bf16[32,5120]{1,0:T(8,128)(2,1)S(1)} %collective-permute-done.11), channel_id=1, source_target_pairs={{0,15},{1,0},{2,1},{3,2},{4,3},{5,4},{6,5},{7,6},{8,7},{9,8},{10,9... | collective-permute-start | bytes 983048 | tf_op jit(solution)/shard_map/ppermute | solution.py:22
  99.7 11.7 %collective-permute-start.6 = (bf16[32,5120]{1,0:T(8,128)(2,1)S(1)}, bf16[32,5120]{1,0:T(8,128)(2,1)}, u32[]{:S(2)}, u32[]{:S(2)}) collective-permute-start(bf16[32,5120]{1,0:T(8,128)(2,1)S(1)} %collective-permute-done.5), channel_id=1, source_target_pairs={{0,1},{1,2},{2,3},{3,4},{4,5},{5,6},{6,7},{7,8},{8,9},{9,10},{10,1... | collective-permute-start | bytes 983048 | tf_op jit(solution)/shard_map/ppermute | solution.py:20
  105.5 11.5 %collective-permute-start.13 = (bf16[32,5120]{1,0:T(8,128)(2,1)}, bf16[32,5120]{1,0:T(8,128)(2,1)}, u32[]{:S(2)}, u32[]{:S(2)}) collective-permute-start(bf16[32,5120]{1,0:T(8,128)(2,1)} %collective-permute-done.12), channel_id=1, source_target_pairs={{0,15},{1,0},{2,1},{3,2},{4,3},{5,4},{6,5},{7,6},{8,7},{9,8},{10,9... | collective-permute-start | bytes 983048 | tf_op jit(solution)/shard_map/ppermute | solution.py:22
  111.4 11.9 %collective-permute-start.7 = (bf16[32,5120]{1,0:T(8,128)(2,1)}, bf16[32,5120]{1,0:T(8,128)(2,1)}, u32[]{:S(2)}, u32[]{:S(2)}) collective-permute-start(bf16[32,5120]{1,0:T(8,128)(2,1)} %collective-permute-done.6), channel_id=1, source_target_pairs={{0,1},{1,2},{2,3},{3,4},{4,5},{5,6},{6,7},{7,8},{8,9},{9,10},{10,1... | collective-permute-start | bytes 983048 | tf_op jit(solution)/shard_map/ppermute | solution.py:20
  117.0 17.2 %collective-permute-start.14 = (bf16[32,5120]{1,0:T(8,128)(2,1)}, bf16[32,5120]{1,0:T(8,128)(2,1)S(1)}, u32[]{:S(2)}, u32[]{:S(2)}) collective-permute-start(bf16[32,5120]{1,0:T(8,128)(2,1)} %collective-permute-done.13), channel_id=1, source_target_pairs={{0,15},{1,0},{2,1},{3,2},{4,3},{5,4},{6,5},{7,6},{8,7},{9,8},{10,9... | collective-permute-start | bytes 983048 | tf_op jit(solution)/shard_map/ppermute | solution.py:22
  158.9 201.8 %all-gather.3.cloned.1.call-start = ((), (), s32[]{:S(2)}) async-start(), calls=%async_computation.3 | async-start | bytes 14745600 | tf_op jit(solution)/shard_map/all_gather | solution.py:199
  159.5 217.1 %all-gather.5.cloned.1.call-start = ((), (), s32[]{:S(2)}) async-start(), calls=%async_computation.4 | async-start | bytes 7372800 | tf_op jit(solution)/shard_map/all_gather | solution.py:200
  238.6 11.7 %collective-permute-start.16 = (bf16[32,5120]{1,0:T(8,128)(2,1)S(1)}, bf16[32,5120]{1,0:T(8,128)(2,1)S(1)}, u32[]{:S(2)}, u32[]{:S(2)}) collective-permute-start(bf16[32,5120]{1,0:T(8,128)(2,1)S(1)} %multiply_convert_fusion.1), channel_id=1, source_target_pairs={{0,1},{1,2},{2,3},{3,4},{4,5},{5,6},{6,7},{7,8},{8,9},{9,10},{10,1... | collective-permute-start | bytes 983048 | tf_op jit(solution)/shard_map/ppermute | solution.py:20
  250.4 10.7 %collective-permute-start.17 = (bf16[32,5120]{1,0:T(8,128)(2,1)S(1)}, bf16[32,5120]{1,0:T(8,128)(2,1)S(1)}, u32[]{:S(2)}, u32[]{:S(2)}) collective-permute-start(bf16[32,5120]{1,0:T(8,128)(2,1)S(1)} %collective-permute-done.16), channel_id=1, source_target_pairs={{0,1},{1,2},{2,3},{3,4},{4,5},{5,6},{6,7},{7,8},{8,9},{9,10},{10,1... | collective-permute-start | bytes 983048 | tf_op jit(solution)/shard_map/ppermute | solution.py:20
  250.4 10.8 %collective-permute-start.24 = (bf16[32,5120]{1,0:T(8,128)(2,1)S(1)}, bf16[32,5120]{1,0:T(8,128)(2,1)S(1)}, u32[]{:S(2)}, u32[]{:S(2)}) collective-permute-start(bf16[32,5120]{1,0:T(8,128)(2,1)S(1)} %multiply_convert_fusion.1), channel_id=1, source_target_pairs={{0,15},{1,0},{2,1},{3,2},{4,3},{5,4},{6,5},{7,6},{8,7},{9,8},{10,9... | collective-permute-start | bytes 983048 | tf_op jit(solution)/shard_map/ppermute | solution.py:22
  261.1 10.4 %collective-permute-start.18 = (bf16[32,5120]{1,0:T(8,128)(2,1)S(1)}, bf16[32,5120]{1,0:T(8,128)(2,1)S(1)}, u32[]{:S(2)}, u32[]{:S(2)}) collective-permute-start(bf16[32,5120]{1,0:T(8,128)(2,1)S(1)} %collective-permute-done.17), channel_id=1, source_target_pairs={{0,1},{1,2},{2,3},{3,4},{4,5},{5,6},{6,7},{7,8},{8,9},{9,10},{10,1... | collective-permute-start | bytes 983048 | tf_op jit(solution)/shard_map/ppermute | solution.py:20
  261.1 10.4 %collective-permute-start.25 = (bf16[32,5120]{1,0:T(8,128)(2,1)S(1)}, bf16[32,5120]{1,0:T(8,128)(2,1)S(1)}, u32[]{:S(2)}, u32[]{:S(2)}) collective-permute-start(bf16[32,5120]{1,0:T(8,128)(2,1)S(1)} %collective-permute-done.24), channel_id=1, source_target_pairs={{0,15},{1,0},{2,1},{3,2},{4,3},{5,4},{6,5},{7,6},{8,7},{9,8},{10,9... | collective-permute-start | bytes 983048 | tf_op jit(solution)/shard_map/ppermute | solution.py:22
  271.5 10.4 %collective-permute-start.19 = (bf16[32,5120]{1,0:T(8,128)(2,1)S(1)}, bf16[32,5120]{1,0:T(8,128)(2,1)S(1)}, u32[]{:S(2)}, u32[]{:S(2)}) collective-permute-start(bf16[32,5120]{1,0:T(8,128)(2,1)S(1)} %collective-permute-done.18), channel_id=1, source_target_pairs={{0,1},{1,2},{2,3},{3,4},{4,5},{5,6},{6,7},{7,8},{8,9},{9,10},{10,1... | collective-permute-start | bytes 983048 | tf_op jit(solution)/shard_map/ppermute | solution.py:20
  271.5 10.4 %collective-permute-start.26 = (bf16[32,5120]{1,0:T(8,128)(2,1)S(1)}, bf16[32,5120]{1,0:T(8,128)(2,1)S(1)}, u32[]{:S(2)}, u32[]{:S(2)}) collective-permute-start(bf16[32,5120]{1,0:T(8,128)(2,1)S(1)} %collective-permute-done.25), channel_id=1, source_target_pairs={{0,15},{1,0},{2,1},{3,2},{4,3},{5,4},{6,5},{7,6},{8,7},{9,8},{10,9... | collective-permute-start | bytes 983048 | tf_op jit(solution)/shard_map/ppermute | solution.py:22
  281.9 10.8 %collective-permute-start.20 = (bf16[32,5120]{1,0:T(8,128)(2,1)S(1)}, bf16[32,5120]{1,0:T(8,128)(2,1)}, u32[]{:S(2)}, u32[]{:S(2)}) collective-permute-start(bf16[32,5120]{1,0:T(8,128)(2,1)S(1)} %collective-permute-done.19), channel_id=1, source_target_pairs={{0,1},{1,2},{2,3},{3,4},{4,5},{5,6},{6,7},{7,8},{8,9},{9,10},{10,1... | collective-permute-start | bytes 983048 | tf_op jit(solution)/shard_map/ppermute | solution.py:20
  292.7 12.0 %collective-permute-start.21 = (bf16[32,5120]{1,0:T(8,128)(2,1)}, bf16[32,5120]{1,0:T(8,128)(2,1)}, u32[]{:S(2)}, u32[]{:S(2)}) collective-permute-start(bf16[32,5120]{1,0:T(8,128)(2,1)} %collective-permute-done.20), channel_id=1, source_target_pairs={{0,1},{1,2},{2,3},{3,4},{4,5},{5,6},{6,7},{7,8},{8,9},{9,10},{10,1... | collective-permute-start | bytes 983048 | tf_op jit(solution)/shard_map/ppermute | solution.py:20
  292.7 171.6 %reduce-scatter.5.cloned.1.call-start = ((), (), s32[]{:S(2)}) async-start(), calls=%async_computation.5 | async-start | bytes 5709824 | tf_op jit(solution)/shard_map/reduce_scatter | solution.py:104
  292.8 41.3 %collective-permute-start.28 = (bf16[32,5120]{1,0:T(8,128)(2,1)S(1)}, bf16[32,5120]{1,0:T(8,128)(2,1)S(1)}, u32[]{:S(2)}, u32[]{:S(2)}) collective-permute-start(bf16[32,5120]{1,0:T(8,128)(2,1)S(1)} %collective-permute-done.27), channel_id=1, source_target_pairs={{0,15},{1,0},{2,1},{3,2},{4,3},{5,4},{6,5},{7,6},{8,7},{9,8},{10,9... | collective-permute-start | bytes 983048 | tf_op jit(solution)/shard_map/ppermute | solution.py:22
  304.7 31.4 %collective-permute-start.22 = (bf16[32,5120]{1,0:T(8,128)(2,1)}, bf16[32,5120]{1,0:T(8,128)(2,1)S(1)}, u32[]{:S(2)}, u32[]{:S(2)}) collective-permute-start(bf16[32,5120]{1,0:T(8,128)(2,1)} %collective-permute-done.21), channel_id=1, source_target_pairs={{0,1},{1,2},{2,3},{3,4},{4,5},{5,6},{6,7},{7,8},{8,9},{9,10},{10,1... | collective-permute-start | bytes 983048 | tf_op jit(solution)/shard_map/ppermute | solution.py:20
  336.2 10.5 %collective-permute-start.23 = (bf16[32,5120]{1,0:T(8,128)(2,1)S(1)}, bf16[32,5120]{1,0:T(8,128)(2,1)S(1)}, u32[]{:S(2)}, u32[]{:S(2)}) collective-permute-start(bf16[32,5120]{1,0:T(8,128)(2,1)S(1)} %collective-permute-done.22), channel_id=1, source_target_pairs={{0,1},{1,2},{2,3},{3,4},{4,5},{5,6},{6,7},{7,8},{8,9},{9,10},{10,1... | collective-permute-start | bytes 983048 | tf_op jit(solution)/shard_map/ppermute | solution.py:20
  341.7 18.3 %collective-permute-start.30 = (bf16[32,5120]{1,0:T(8,128)(2,1)S(1)}, bf16[32,5120]{1,0:T(8,128)(2,1)S(1)}, u32[]{:S(2)}, u32[]{:S(2)}) collective-permute-start(bf16[32,5120]{1,0:T(8,128)(2,1)S(1)} %collective-permute-done.29), channel_id=1, source_target_pairs={{0,15},{1,0},{2,1},{3,2},{4,3},{5,4},{6,5},{7,6},{8,7},{9,8},{10,9... | collective-permute-start | bytes 983048 | tf_op jit(solution)/shard_map/ppermute | solution.py:22
  (51 other events, 1697.2 us)
Sparse Core Ops, SparseCore 0:
  159.1 77.8 reduce-scatter.2
  386.9 77.3 reduce-scatter.4
Sparse Core Ops, SparseCore 1:
  161.1 68.1 all-gather.2
  292.8 43.2 all-gather.4
